TPU v7x, 256 devices: a whole 4x4x8 slice. The times are simulated.
256 devices in a mesh: req: 32 (over z_hi, y, core), tp: 8 (over x, z_lo).
Axes of the slice: x: 4, y: 4, z: 8 (z_hi: 4, z_lo: 2; z = z_hi * 2 + z_lo), core: 2. Of those that a mesh axis runs over, the one named last changes fastest.
Arguments:
- hidden_in: bfloat16 [4096, 5120], P('req', 'tp'), may hold values from -6 to 6
- norm_gain: bfloat16 [5120], P('tp'), may hold values from 0.099609375 to 1.8984375
- q_weight: bfloat16 [5120, 3072], P(None, 'tp'), may hold values from -0.078125 to 0.078125
- q_bias: bfloat16 [3072], P('tp'), may hold values from -4 to 4
- k_weight: bfloat16 [5120, 1024], P(None, 'tp'), may hold values from -0.125 to 0.125
- k_bias: bfloat16 [1024], P('tp'), may hold values from -5 to 5
- v_weight: bfloat16 [5120, 1024], P(None, 'tp'), may hold values from -0.3125 to 0.3125
- v_bias: bfloat16 [1024], P('tp'), may hold values from -10 to 10
- o_weight: bfloat16 [3072, 5120], P('tp'), may hold values from -0.3125 to 0.3125
- prefix_kv: bfloat16 [32768, 2, 1024], P('req', None, 'tp'), as said below
- suffix_len: int32 [32], P('req'), may hold values from 18 to 128, as said below
- req_prefix: int32 [32], P('req'), may hold values from 0 to 3, as said below
- block_owner: int32 [32], replicated, may hold values from 0 to 31, each once
Outputs:
- attn_out: bfloat16 [4096, 5120], P('req', 'tp')
Inputs may be any that keep to these rules, and one draw needn't show every extreme that they name: `suffix_len`: suffix tokens of each request; some request has exactly 128 and some exactly 18. `req_prefix`: every prefix is continued by exactly 8 requests. Block j of prefix p is held by req index block_owner[p * 8 + j]; each req index holds one block. `prefix_kv`: cached keys already carry the rotary embedding of their prefix positions.
All inputs are finite; a program needn't handle non-finite values.
Results may differ from a plain program's by a relative error of at most 0.022.
Values may be sent and summed in bfloat16 or wider, within the bound.
No kernel may reach another device: no remote copies, remote signals or barrier semaphores. Data moves between devices by JAX's collectives and lax.ppermute only.
A program may use at most 128 MiB of HBM per device.

v0:
```python
import jax
import jax.numpy as jnp
from jax import lax
from jax.sharding import PartitionSpec as P

HD = 128
NPREF = 4
THETA = 1000000.0
EPSILON = 1e-06


def rotate(heads, positions):
    half = HD // 2
    freqs = THETA ** (-(jnp.arange(half, dtype=jnp.float32) * 2.0) / HD)
    angles = positions.astype(jnp.float32)[:, None] * freqs[None, :]
    cosine = jnp.cos(angles)[:, None, :]
    sine = jnp.sin(angles)[:, None, :]
    first = heads[..., :half]
    second = heads[..., half:]
    return jnp.concatenate(
        [first * cosine - second * sine, second * cosine + first * sine], axis=-1
    )


def block_stats(grouped, keys, values, allowed):
    scores = jnp.einsum(
        "sghd,kgd->sghk", grouped, keys, preferred_element_type=jnp.float32
    ) * HD ** (-0.5)
    if allowed is not None:
        scores = jnp.where(allowed[:, None, None, :], scores, -jnp.inf)
    peak = jnp.max(scores, axis=-1)
    weights = jnp.exp(scores - peak[..., None])
    total = jnp.sum(weights, axis=-1)
    mixed = jnp.einsum(
        "sghk,kgd->sghd", weights.astype(jnp.bfloat16), values, preferred_element_type=jnp.float32
    )
    return (peak, total, mixed)


def combine(first, second):
    peak = jnp.maximum(first[0], second[0])
    left = jnp.exp(first[0] - peak)
    right = jnp.exp(second[0] - peak)
    total = first[1] * left + second[1] * right
    mixed = first[2] * left[..., None] + second[2] * right[..., None]
    return (peak, total, mixed)


def shards(
    hidden_in,
    norm_gain,
    q_weight,
    q_bias,
    k_weight,
    k_bias,
    v_weight,
    v_bias,
    o_weight,
    prefix_kv,
    suffix_len,
    req_prefix,
    block_owner,
):
    length = hidden_in.shape[0]
    devices = lax.axis_size("req")
    owned = devices // NPREF
    block = prefix_kv.shape[0]
    prefix_len = block * owned
    kv_heads = k_weight.shape[1] // HD
    q_heads = q_weight.shape[1] // HD
    group = q_heads // kv_heads
    full, gain = (
        lax.all_gather(hidden_in, "tp", axis=1, tiled=True),
        lax.all_gather(norm_gain, "tp", axis=0, tiled=True),
    )
    tokens = full.astype(jnp.float32)
    meansq = jnp.mean(tokens * tokens, axis=-1, keepdims=True)
    normed = (tokens * lax.rsqrt(meansq + EPSILON) * gain.astype(jnp.float32)).astype(jnp.bfloat16)
    positions = prefix_len + jnp.arange(length, dtype=jnp.int32)
    queries = jnp.dot(normed, q_weight, preferred_element_type=jnp.float32) + q_bias.astype(
        jnp.float32
    )
    queries = rotate(queries.reshape(length, q_heads, HD), positions).astype(jnp.bfloat16)
    queries = queries.reshape(length, kv_heads, group, HD)
    keys = jnp.dot(normed, k_weight, preferred_element_type=jnp.float32) + k_bias.astype(
        jnp.float32
    )
    keys = rotate(keys.reshape(length, kv_heads, HD), positions).astype(jnp.bfloat16)
    values = jnp.dot(normed, v_weight, preferred_element_type=jnp.float32) + v_bias.astype(
        jnp.float32
    )
    values = values.astype(jnp.bfloat16).reshape(length, kv_heads, HD)
    slot_index = jnp.arange(length, dtype=jnp.int32)
    causal = slot_index[None, :] <= slot_index[:, None]
    state = block_stats(queries, keys, values, causal)
    which = req_prefix[0]

    def advance(current, cached):
        return (combine(current, block_stats(queries, cached[:, 0], cached[:, 1], None)), None)

    everything = lax.all_gather(prefix_kv, "req", axis=0, tiled=True)
    stacked = everything.reshape(devices, block, 2, kv_heads, HD)
    owners = lax.dynamic_slice_in_dim(block_owner, which * owned, owned)
    chosen = jnp.take(stacked, owners, axis=0)
    state, unused = lax.scan(advance, state, chosen)
    peak, total, mixed = state
    context = (mixed / total[..., None]).astype(jnp.bfloat16).reshape(length, q_heads * HD)
    partial_value = jnp.dot(context, o_weight, preferred_element_type=jnp.float32)
    summed = lax.psum_scatter(
        partial_value.astype(jnp.bfloat16), "tp", scatter_dimension=1, tiled=True
    ).astype(jnp.float32)
    valid = slot_index < suffix_len[0]
    return jnp.where(valid[:, None], summed, jnp.float32(0.0)).astype(jnp.bfloat16)


def solution(mesh):
    placed = (
        P("req", "tp"),
        P("tp"),
        P(None, "tp"),
        P("tp"),
        P(None, "tp"),
        P("tp"),
        P(None, "tp"),
        P("tp"),
        P("tp", None),
        P("req", None, "tp"),
        P("req"),
        P("req"),
        P(),
    )
    return jax.shard_map(
        shards, mesh=mesh, in_specs=placed, out_specs=P("req", "tp"), check_vma=False
    )
```

profile of v0, /device:TPU:8, one launch (start us, length us, event | category | flops | bytes accessed | tf_op | source)
XLA Modules:
  0.0 277.1 jit_solution(18251878204632939527)
XLA Ops:
  6.6 0.0 all-gather.4.cloned.1.call-start
  6.6 0.7 all-gather.4.cloned.1.call-update
  7.3 0.0 all-gather.6.cloned.1.call-start
  7.3 1.9 copy.47
  9.3 0.0 reduce-scatter.4.cloned.1.call-start
  9.3 28.0 %all-gather = bf16[8,1,640]{2,1,0:T(2,128)(2,1)S(1)} all-gather(bf16[1,1,640]{2,1,0:T(2,128)(2,1)S(1)} %reshape.278), channel_id=1, replica_groups=mesh['req'=32,'tp'=8] {'tp'}, dimensions={0}, use_global_device_ids=true | all-gather | bytes 11520 | tf_op jit(solution)/shard_map/all_gather | solution.py:74
  38.2 0.1 compare_and_fusion
  38.3 0.3 multiply_cosine_fusion
  38.6 18.3 %all-gather.4.cloned.1.call-done = bf16[128,5120]{1,0:T(8,128)(2,1)} async-done(((bf16[128,640]{1,0:T(8,128)(2,1)}), bf16[128,5120]{1,0:T(8,128)(2,1)}) %all-gather.4.cloned.1.call-update) | async-done | bytes 1310736 | tf_op jit(solution)/shard_map/all_gather | solution.py:73
  56.9 1.6 fusion.15
  58.5 3.4 %convolution_add_fusion = f32[128,384]{1,0:T(8,128)S(1)} fusion(bf16[5120,384]{1,0:T(8,128)(2,1)} %param.17, f32[384]{0:T(512)S(1)} %convert_element_type.79, bf16[128,5120]{1,0:T(8,128)(2,1)} %all-gather.4.cloned.1.call-done, f32[5120]{0:T(1024)S(1)} %bitcast.155, f32[128]{0:T(128)S(1)} %add_rsqrt_fusion), kind=kOutput, calls=%fused_computation.36 | convolution fusion | flops 505987072 | bytes 5462016 | tf_op jit(solution)/shard_map/dot_general | solution.py:80
  62.0 0.1 copy.41
  62.1 0.1 copy.60
  62.3 0.1 copy.61
  62.4 0.1 subtract_convert_fusion
  62.5 0.1 pad_maximum_fusion
  62.6 0.7 copy-done.1
  63.3 2.1 fusion.20
  65.4 0.2 fusion.43
  65.6 0.3 fusion.50
  65.9 0.1 fusion.24
  65.9 0.8 convolution_bitcast_fusion.1
  66.7 96.2 %all-gather.6.cloned.1.call-done = bf16[32768,2,128]{2,0,1:T(8,128)(2,1)} async-done(((bf16[1024,2,128]{2,0,1:T(8,128)(2,1)}), bf16[32768,2,128]{2,0,1:T(8,128)(2,1)}) %all-gather.6.cloned.1.call-update) | async-done | bytes 16777232 | tf_op jit(solution)/shard_map/all_gather | solution.py:101
  162.9 13.8 %copy.48 = bf16[32,1024,2,128]{3,1,2,0:T(8,128)(2,1)} copy(bf16[32,1024,2,128]{3,1,0,2:T(8,128)(2,1)} %bitcast.145) | data formatting | bytes 33554432 | tf_op jit(solution)/shard_map/reshape | solution.py:102
  176.6 8.8 %gather_fusion = bf16[8,1024,2,128]{3,1,2,0:T(8,128)(2,1)} fusion(bf16[32,1024,2,128]{3,1,2,0:T(8,128)(2,1)} %copy.48, s32[1024]{0:T(1024)S(1)} %pad_clamp_fusion), kind=kCustom, calls=%fused_computation | custom fusion | bytes 8388640 | tf_op jit(solution)/shard_map/jit(_take)/gather | solution.py:104
  185.4 4.6 %fusion.14 = bf16[8,1024,2,1,128]{4,1,2,3,0:T(8,128)(2,1)} fusion(bf16[8,1024,2,128]{3,1,2,0:T(8,128)(2,1)} %gather_fusion, pred[8]{0:T(512)(128)(4,1)S(1)} %get-tuple-element.72), kind=kLoop, calls=%fused_computation.27 | loop fusion | flops 2097152 | bytes 8388616 | tf_op jit(solution)/shard_map/while | solution.py:105
  190.0 17.9 %while.14 = (s32[]{:T(128)}, f32[128,1,3]{0,2,1:T(4,128)S(1)}, f32[128,1,3]{0,2,1:T(4,128)S(1)}, f32[128,1,3,128]{0,3,2,1:T(8,128)S(1)}, bf16[8,1024,2,1,128]{4,...) while((s32[]{:T(128)}, f32[128,1,3]{0,2,1:T(4,128)S(1)}, f32[128,1,3]{0,2,1:T(4,128)S(1)}, ...), condition=%wide.region_6.7_spmd, body=%wide.region_3.0_spmd.sunk | while | flops 203835264 | bytes 6813777 | solution.py:105
  190.0 1.1 dynamic-slice_bitcast_fusion.2
  191.1 0.4 bitcast_reduce_fusion.2
  191.5 0.2 fusion.63
  191.7 0.5 fusion.65
  192.3 1.1 dynamic-slice_bitcast_fusion.2
  193.3 0.4 bitcast_reduce_fusion.2
  193.7 0.2 fusion.63
  194.0 0.5 fusion.65
  194.5 1.1 dynamic-slice_bitcast_fusion.2
  195.6 0.4 bitcast_reduce_fusion.2
  196.0 0.2 fusion.63
  196.2 0.5 fusion.65
  196.7 1.1 dynamic-slice_bitcast_fusion.2
  197.8 0.4 bitcast_reduce_fusion.2
  198.2 0.2 fusion.63
  198.5 0.5 fusion.65
  199.0 1.1 dynamic-slice_bitcast_fusion.2
  200.1 0.4 bitcast_reduce_fusion.2
  200.4 0.2 fusion.63
  200.7 0.5 fusion.65
  201.2 1.1 dynamic-slice_bitcast_fusion.2
  202.3 0.4 bitcast_reduce_fusion.2
  202.7 0.2 fusion.63
  202.9 0.5 fusion.65
  203.5 1.1 dynamic-slice_bitcast_fusion.2
  204.5 0.4 bitcast_reduce_fusion.2
  204.9 0.2 fusion.63
  205.2 0.5 fusion.65
  205.7 1.1 dynamic-slice_bitcast_fusion.2
  206.8 0.4 bitcast_reduce_fusion.2
  207.2 0.2 fusion.63
  207.4 0.5 fusion.65
  208.0 3.0 %convolution_convert_fusion = bf16[128,5120]{1,0:T(8,128)(2,1)S(1)} fusion(bf16[128,384]{0,1:T(8,128)(2,1)S(1)} %bitcast.150, bf16[384,5120]{1,0:T(8,128)(2,1)} %param.23), kind=kOutput, calls=%fused_computation.25 | convolution fusion | flops 503971840 | bytes 5341184 | tf_op jit(solution)/shard_map/dot_general | solution.py:108
  211.0 1.4 copy.58
  213.1 55.6 %reduce-scatter.4.cloned.1.call-done = bf16[640,128]{1,0:T(8,128)(2,1)} async-done(((bf16[5120,128]{1,0:T(8,128)(2,1)}), bf16[640,128]{1,0:T(8,128)(2,1)}) %reduce-scatter.4.cloned.1.call-update) | async-done | bytes 163856
  268.7 1.1 copy.59
  269.8 0.8 select_convert_fusion
  (52 shorter events, 0.4 us)
Async XLA Ops:
  6.5 59.4 %copy-start = (bf16[5120,128]{1,0:T(8,128)(2,1)S(1)}, bf16[5120,128]{1,0:T(8,128)(2,1)}, u32[]{:S(2)}) copy-start(bf16[5120,128]{1,0:T(8,128)(2,1)} %param.21) | copy-start | bytes 3932164
  6.5 2.8 %copy-start.2 = (bf16[640]{0:T(1024)(128)(2,1)S(1)}, bf16[640]{0:T(1024)(128)(2,1)}, u32[]{:S(2)}) copy-start(bf16[640]{0:T(1024)(128)(2,1)} %param.16) | copy-start | bytes 3844
  6.5 30.9 %copy-start.3 = (bf16[384]{0:T(512)(128)(2,1)S(1)}, bf16[384]{0:T(512)(128)(2,1)}, u32[]{:S(2)}) copy-start(bf16[384]{0:T(512)(128)(2,1)} %param.18) | copy-start | bytes 2308
  6.5 30.9 %copy-start.5 = (bf16[128]{0:T(256)(128)(2,1)S(1)}, bf16[128]{0:T(256)(128)(2,1)}, u32[]{:S(2)}) copy-start(bf16[128]{0:T(256)(128)(2,1)} %param.20) | copy-start | bytes 772
  6.5 30.9 %copy-start.6 = (bf16[128]{0:T(256)(128)(2,1)S(1)}, bf16[128]{0:T(256)(128)(2,1)}, u32[]{:S(2)}) copy-start(bf16[128]{0:T(256)(128)(2,1)} %param.22) | copy-start | bytes 772
  6.5 31.6 %copy-start.4 = (s32[32]{0:T(128)S(1)}, s32[32]{0:T(128)}, u32[]{:S(2)}) copy-start(s32[32]{0:T(128)} %param.27) | copy-start | bytes 388
  6.6 50.3 %all-gather.4.cloned.1.call-start = ((), (), s32[]{:S(2)}) async-start(), calls=%async_computation.1 | async-start | bytes 1474560 | tf_op jit(solution)/shard_map/all_gather | solution.py:73
  7.3 155.6 %all-gather.6.cloned.1.call-start = ((), (), s32[]{:S(2)}) async-start(), calls=%async_computation.2 | async-start | bytes 17301504 | tf_op jit(solution)/shard_map/all_gather | solution.py:101
  9.3 259.5 %reduce-scatter.4.cloned.1.call-start = ((), (), s32[]{:S(2)}) async-start(), calls=%async_computation.3 | async-start | bytes 1474560
  62.0 1.3 copy-start.1
Sparse Core Ops, SparseCore 0:
  9.2 47.6 all-gather.3
  59.5 103.3 all-gather.5
  212.6 56.1 reduce-scatter.3
where the time goes:
time: 278 us; the launch traced here: 277 us
  waiting for transfers between devices  171 us (62%)
  local copies, waits for them, and re-layouts  36.8 us (13%)
  blocking collectives  28 us (10%)
  matrix products  16.4 us (6%)
  between operations  14.6 us (5%)
  other arithmetic  9.93 us (4%)
    all_gather x1, waiting for transfers between devices, shards(): everything = lax.all_gather(prefix_kv, 'req', axis=0, tiled=True)  96.2 us
    unnamed x4, waiting for transfers between devices  56.4 us
    all_gather x1, blocking collectives, shards(): lax.all_gather(norm_gain, 'tp', axis=0, tiled=True)  28 us
    all_gather x1, waiting for transfers between devices, shards(): lax.all_gather(hidden_in, 'tp', axis=1, tiled=True)  18.3 us
    reshape x1, local copies, waits for them, and re-layouts, shards(): stacked = everything.reshape(devices, block, 2, kv_heads, HD)  13.8 us
    gather x1, local copies, waits for them, and re-layouts, shards(): chosen = jnp.take(stacked, owners, axis=0)  8.79 us
    squeeze x8, local copies, waits for them, and re-layouts, shards(): state, unused = lax.scan(advance, state, chosen)  8.64 us
  transfers between devices with their start and end apart: 3, of which 3 were waited for; matrix products, arithmetic and copies ran while one was open for 4% of the time, Pallas kernels for 0%

commit v1 on v0

--- a/solution.py
+++ b/solution.py
@@ -98,7 +98,9 @@
     def advance(current, cached):
         return (combine(current, block_stats(queries, cached[:, 0], cached[:, 1], None)), None)
 
-    everything = lax.all_gather(prefix_kv, "req", axis=0, tiled=True)
+    everything = jnp.concatenate(
+        lax.all_to_all(jnp.stack([prefix_kv] * lax.axis_size("req")), "req", 0, 0), axis=0
+    )
     stacked = everything.reshape(devices, block, 2, kv_heads, HD)
     owners = lax.dynamic_slice_in_dim(block_owner, which * owned, owned)
     chosen = jnp.take(stacked, owners, axis=0)

time: 278 us -> 537 us (1.93)
  blocking collectives: 28 us -> 406 us
  waiting for transfers between devices: 171 us -> 48.5 us
  starting transfers between devices: 0.12 us -> 12 us
  local copies, waits for them, and re-layouts: 36.8 us -> 28.5 us
    all_gather x1, blocking collectives: 28 us -> 406 us  [shards(): lax.all_gather(norm_gain, 'tp', axis=0, tiled=True)]
    all_gather x1 -> x0, waiting for transfers between devices: 96.2 us -> none  [shards(): everything = lax.all_gather(prefix_kv, 'req', axis=0, tiled=True)]
    all_gather x1, waiting for transfers between devices: 18.3 us -> 0.02 us  [shards(): lax.all_gather(hidden_in, 'tp', axis=1, tiled=True)]
    reshape x1 -> x0, local copies, waits for them, and re-layouts: 13.8 us -> none  [shards(): stacked = everything.reshape(devices, block, 2, kv_heads, HD)]
    all_to_all x0 -> x1, starting transfers between devices: none -> 11.9 us  [shards(): lax.all_to_all(jnp.stack([prefix_kv] * lax.axis_size('req')), 'req', 0, 0)]
    unnamed x4 -> x3, waiting for transfers between devices: 56.4 us -> 48.5 us
    another operation x0 -> x1, local copies, waits for them, and re-layouts: none -> 6.17 us  [shards(): jnp.stack([prefix_kv] * lax.axis_size('req'))]
  transfers between devices with their start and end apart: 3 -> 3, of which waited for: 3 -> 1; matrix products, arithmetic and copies ran while one was open for 4% -> 2% of each run, Pallas kernels for 0% -> 0%
where the time goes in v1:
time: 537 us; the launch traced here: 536 us
  blocking collectives  406 us (76%)
  waiting for transfers between devices  48.5 us (9%)
  local copies, waits for them, and re-layouts  28.5 us (5%)
  matrix products  16.5 us (3%)
  between operations  15 us (3%)
  starting transfers between devices  12 us (2%)
  other arithmetic  9.94 us (2%)
    all_gather x1, blocking collectives, shards(): lax.all_gather(norm_gain, 'tp', axis=0, tiled=True)  406 us
    unnamed x3, waiting for transfers between devices  48.5 us
    all_to_all x1, starting transfers between devices, shards(): lax.all_to_all(jnp.stack([prefix_kv] * lax.axis_size('req')), 'req', 0, 0)  11.9 us
  transfers between devices with their start and end apart: 3, of which 1 were waited for; matrix products, arithmetic and copies ran while one was open for 2% of the time, Pallas kernels for 0%

profile of v1, /device:TPU:8, one launch (start us, length us, event | category | flops | bytes accessed | tf_op | source)
XLA Modules:
  0.0 536.5 jit_solution(6439189096720914906)
XLA Ops:
  6.5 1.2 copy.37
  7.8 6.2 %stack.2 = bf16[32,1024,2,128]{3,1,2,0:T(8,128)(2,1)} broadcast(bf16[1024,2,128]{2,0,1:T(8,128)(2,1)S(1)} %copy.37), dimensions={1,2,3} | broadcast | bytes 17301504 | tf_op jit(solution)/shard_map/stack | solution.py:102
  13.9 11.9 %all-to-all-start = ((bf16[32,1024,2,128]{3,1,2,0:T(8,128)(2,1)}), bf16[32,1024,2,128]{3,1,2,0:T(8,128)(2,1)}, u32[]{:S(2)}, u32[]{:S(2)}) async-start(bf16[32,1024,2,128]{3,1,2,0:T(8,128)(2,1)} %stack.2), calls=%async_computation | async-start | bytes 33554432 | tf_op jit(solution)/shard_map/all_to_all | solution.py:102
  25.9 0.0 all-gather.3.cloned.1.call-start
  25.9 0.7 all-gather.3.cloned.1.call-update
  26.6 0.0 reduce-scatter.4.cloned.1.call-start
  26.7 405.8 %all-gather = bf16[8,1,640]{2,1,0:T(2,128)(2,1)S(1)} all-gather(bf16[1,1,640]{2,1,0:T(2,128)(2,1)S(1)} %reshape.276), channel_id=1, replica_groups=mesh['req'=32,'tp'=8] {'tp'}, dimensions={0}, use_global_device_ids=true | all-gather | bytes 11520 | tf_op jit(solution)/shard_map/all_gather | solution.py:74
  433.2 0.1 compare_and_fusion
  433.3 0.3 multiply_cosine_fusion
  433.6 0.0 all-gather.3.cloned.1.call-done
  433.6 1.7 fusion.15
  435.3 3.4 convolution_add_fusion
  438.7 0.1 copy.31
  438.9 0.1 copy.49
  439.0 0.1 copy.50
  439.2 0.1 subtract_convert_fusion
  439.2 0.1 pad_maximum_fusion
  439.3 0.7 copy-done.1
  440.1 2.1 fusion.20
  442.1 0.2 fusion.43
  442.3 0.3 fusion.50
  442.6 0.1 fusion.24
  442.7 0.8 convolution_bitcast_fusion.1
  443.5 8.8 %gather_fusion = bf16[8,1024,2,128]{3,1,2,0:T(8,128)(2,1)} fusion(bf16[32,1024,2,128]{3,1,2,0:T(8,128)(2,1)} %all-to-all-done, s32[1024]{0:T(1024)S(1)} %pad_clamp_fusion), kind=kCustom, calls=%fused_computation | custom fusion | bytes 8388640 | tf_op jit(solution)/shard_map/jit(_take)/gather | solution.py:106
  452.3 4.6 fusion.14
  456.9 18.0 %while.14 = (s32[]{:T(128)}, f32[128,1,3]{0,2,1:T(4,128)S(1)}, f32[128,1,3]{0,2,1:T(4,128)S(1)}, f32[128,1,3,128]{0,3,2,1:T(8,128)S(1)}, bf16[8,1024,2,1,128]{4,...) while((s32[]{:T(128)}, f32[128,1,3]{0,2,1:T(4,128)S(1)}, f32[128,1,3]{0,2,1:T(4,128)S(1)}, ...), condition=%wide.region_6.7_spmd, body=%wide.region_3.0_spmd.sunk | while | flops 203835264 | bytes 6813777 | solution.py:107
  456.9 1.1 dynamic-slice_bitcast_fusion.2
  457.9 0.4 bitcast_reduce_fusion.2
  458.3 0.2 fusion.63
  458.6 0.5 fusion.65
  459.1 1.1 dynamic-slice_bitcast_fusion.2
  460.2 0.4 bitcast_reduce_fusion.2
  460.6 0.2 fusion.63
  460.8 0.5 fusion.65
  461.4 1.1 dynamic-slice_bitcast_fusion.2
  462.4 0.4 bitcast_reduce_fusion.2
  462.8 0.2 fusion.63
  463.1 0.5 fusion.65
  463.6 1.1 dynamic-slice_bitcast_fusion.2
  464.7 0.4 bitcast_reduce_fusion.2
  465.1 0.2 fusion.63
  465.3 0.5 fusion.65
  465.8 1.1 dynamic-slice_bitcast_fusion.2
  466.9 0.4 bitcast_reduce_fusion.2
  467.3 0.2 fusion.63
  467.6 0.5 fusion.65
  468.1 1.1 dynamic-slice_bitcast_fusion.2
  469.2 0.4 bitcast_reduce_fusion.2
  469.6 0.2 fusion.63
  469.8 0.5 fusion.65
  470.3 1.1 dynamic-slice_bitcast_fusion.2
  471.4 0.4 bitcast_reduce_fusion.2
  471.8 0.2 fusion.63
  472.1 0.5 fusion.65
  472.6 1.1 dynamic-slice_bitcast_fusion.2
  473.7 0.4 bitcast_reduce_fusion.2
  474.1 0.2 fusion.63
  474.3 0.5 fusion.65
  474.9 3.0 convolution_convert_fusion
  477.9 1.4 copy.47
  479.3 0.0 reduce-scatter.4.cloned.1.call-update
  480.0 47.8 %reduce-scatter.4.cloned.1.call-done = bf16[640,128]{1,0:T(8,128)(2,1)} async-done(((bf16[5120,128]{1,0:T(8,128)(2,1)}), bf16[640,128]{1,0:T(8,128)(2,1)}) %reduce-scatter.4.cloned.1.call-update) | async-done | bytes 163856
  527.8 1.1 copy.48
  528.8 0.8 select_convert_fusion
  (51 shorter events, 0.4 us)
Async XLA Ops:
  6.5 436.1 %copy-start = (bf16[5120,128]{1,0:T(8,128)(2,1)S(1)}, bf16[5120,128]{1,0:T(8,128)(2,1)}, u32[]{:S(2)}) copy-start(bf16[5120,128]{1,0:T(8,128)(2,1)} %param.21) | copy-start | bytes 3932164
  13.9 12.7 %copy-start.2 = (bf16[640]{0:T(1024)(128)(2,1)S(1)}, bf16[640]{0:T(1024)(128)(2,1)}, u32[]{:S(2)}) copy-start(bf16[640]{0:T(1024)(128)(2,1)} %param.16) | copy-start | bytes 3844
  13.9 418.5 %copy-start.3 = (bf16[384]{0:T(512)(128)(2,1)S(1)}, bf16[384]{0:T(512)(128)(2,1)}, u32[]{:S(2)}) copy-start(bf16[384]{0:T(512)(128)(2,1)} %param.18) | copy-start | bytes 2308
  13.9 418.5 %copy-start.5 = (bf16[128]{0:T(256)(128)(2,1)S(1)}, bf16[128]{0:T(256)(128)(2,1)}, u32[]{:S(2)}) copy-start(bf16[128]{0:T(256)(128)(2,1)} %param.20) | copy-start | bytes 772
  13.9 418.6 %copy-start.6 = (bf16[128]{0:T(256)(128)(2,1)S(1)}, bf16[128]{0:T(256)(128)(2,1)}, u32[]{:S(2)}) copy-start(bf16[128]{0:T(256)(128)(2,1)} %param.22) | copy-start | bytes 772
  13.9 419.2 %copy-start.4 = (s32[32]{0:T(128)S(1)}, s32[32]{0:T(128)}, u32[]{:S(2)}) copy-start(s32[32]{0:T(128)} %param.27) | copy-start | bytes 388
  13.9 429.5 %all-to-all-start = ((bf16[32,1024,2,128]{3,1,2,0:T(8,128)(2,1)}), bf16[32,1024,2,128]{3,1,2,0:T(8,128)(2,1)}, u32[]{:S(2)}, u32[]{:S(2)}) async-start(bf16[32,1024,2,128]{3,1,2,0:T(8,128)(2,1)} %stack.2), calls=%async_computation | async-start | bytes 33554432 | tf_op jit(solution)/shard_map/all_to_all | solution.py:102
  25.9 407.8 %all-gather.3.cloned.1.call-start = ((), (), s32[]{:S(2)}) async-start(), calls=%async_computation.2 | async-start | bytes 1474560 | tf_op jit(solution)/shard_map/all_gather | solution.py:73
  26.6 501.2 %reduce-scatter.4.cloned.1.call-start = ((), (), s32[]{:S(2)}) async-start(), calls=%async_computation.3 | async-start | bytes 1474560
  438.7 1.3 copy-start.1
Sparse Core Ops, SparseCore 0:
  28.5 169.3 all-gather.2
  479.5 48.2 reduce-scatter.3
